TPU v7x, 256 devices: a whole 4x4x8 slice. The times are simulated.
256 devices in a mesh: ctx: 16 (over z, core), tp: 16 (over x, y).
Axes of the slice: x: 4, y: 4, z: 8, core: 2. Of those that a mesh axis runs over, the one named last changes fastest.
Arguments:
- q_act: bfloat16 [64, 128, 4096], P('ctx', None, 'tp'), may hold values from -16 to 16
- k_act: bfloat16 [64, 128, 4096], P('ctx', None, 'tp'), may hold values from -16 to 16
- v_act: bfloat16 [64, 128, 4096], P('ctx', None, 'tp'), may hold values from -6 to 6
- grad_out: bfloat16 [8192, 4096], P(('ctx', 'tp')), may hold values from -24 to 24
- w_out: bfloat16 [4096, 4096], P(None, 'tp'), may hold values from -0.09375 to 0.09375
- nbr_tiles: int32 [64, 12], replicated, may hold values from 0 to 63, as said below
- nbr_valid: int32 [64, 12], replicated, may hold values from 0 to 1, as said below
- slot_of: int32 [64], replicated, may hold values from 0 to 63, as said below
Outputs:
- grad_q: bfloat16 [64, 128, 4096], P('ctx', None, 'tp')
- grad_k: bfloat16 [64, 128, 4096], P('ctx', None, 'tp')
- grad_v: bfloat16 [64, 128, 4096], P('ctx', None, 'tp')
- grad_w_out: bfloat16 [4096, 4096], P('ctx', 'tp')
Inputs may be any that keep to these rules, and one draw needn't show every extreme that they name: `nbr_tiles`: row t lists scenario tiles linked to tile t; the live entries of a row name distinct tiles, one of them t itself. `nbr_valid`: every row has at least one live entry; a tile is named by live entries of at most 12 rows. `slot_of`: a permutation; slots c * 4 to c * 4 + 3 are held by index c of ctx.
All inputs are finite; a program needn't handle non-finite values.
Results may differ from a plain program's by a relative error of at most 0.024.
Values may be sent and summed in bfloat16 or wider, within the bound.
No kernel may reach another device: no remote copies, remote signals or barrier semaphores. Data moves between devices by JAX's collectives and lax.ppermute only.
A program may use at most 128 MiB of HBM per device.

v0:
```python
import math
import jax
import jax.numpy as jnp
from jax import lax
from jax.sharding import Mesh
from jax.sharding import PartitionSpec as P

HD = 128
CORES = 2


def slot_tables(nbr_tiles, nbr_valid, slot_of):
    tile_count = slot_of.shape[0]
    slot_index = jnp.arange(tile_count, dtype=jnp.int32)
    matches = (slot_of[:, None] == slot_index[None, :]).astype(jnp.int32)
    near_tiles = jnp.einsum("ts,tj->sj", matches, nbr_tiles)
    live_mask = jnp.einsum("ts,tj->sj", matches, nbr_valid)
    found = (near_tiles[:, :, None] == slot_index[None, None, :]).astype(jnp.int32)
    key_slot = jnp.sum(found * slot_of[None, None, :], axis=2)
    return (key_slot, live_mask)


def to_head(arrays, local_tiles, tile_len, heads_here):
    stacked = jnp.stack([a.reshape(local_tiles, tile_len, heads_here, HD) for a in arrays], axis=1)
    moved = lax.all_to_all(stacked, "core", split_axis=3, concat_axis=0, tiled=True)
    return moved.reshape(local_tiles * heads_here, len(arrays), tile_len, HD)


def from_head(arrays, local_tiles, tile_len, heads_here):
    stacked = jnp.stack(arrays, axis=1)[:, :, :, None, :]
    moved = lax.all_to_all(stacked, "core", split_axis=0, concat_axis=3, tiled=True)
    return tuple(
        (moved[:, n].reshape(local_tiles, tile_len, heads_here * HD) for n in range(len(arrays)))
    )


def ring_gather(x, axis, count):
    ahead = [(i, (i - 1) % count) for i in range(count)]
    behind = [(i, (i + 1) % count) for i in range(count)]
    half = count // 2
    later = [x]
    earlier = []
    down = x
    up = x
    for _ in range(1, half):
        down = lax.ppermute(down, axis, ahead)
        up = lax.ppermute(up, axis, behind)
        later.append(down)
        earlier.append(up)
    if count % 2 == 0 and count > 1:
        cut = x.shape[0] // 2
        first = lax.ppermute(up[:cut], axis, behind)
        second = lax.ppermute(down[cut:], axis, ahead)
        later.append(jnp.concatenate([first, second], axis=0))
    return jnp.concatenate(later + earlier[::-1], axis=0)


def ring_index(slots, own, chip_tiles, count):
    return (slots // chip_tiles - own) % count * chip_tiles + slots % chip_tiles


def per_device(q_act, k_act, v_act, grad_out, w_out, nbr_tiles, nbr_valid, slot_of):
    local_tiles, tile_len, col_width = q_act.shape
    heads_here = col_width // HD
    score_scale = 1.0 / math.sqrt(HD)
    chip_tiles = local_tiles * heads_here
    z_count = lax.axis_size("z")
    own_z = lax.axis_index("z")
    first_slot = own_z * chip_tiles
    key_slot, live_mask = slot_tables(nbr_tiles, nbr_valid, slot_of)
    tile_count = key_slot.shape[0]
    list_len = key_slot.shape[1]
    near_slots = lax.dynamic_slice_in_dim(key_slot, first_slot, chip_tiles, 0)
    near_live = lax.dynamic_slice_in_dim(live_mask, first_slot, chip_tiles, 0)
    full_rows = lax.all_gather(grad_out, "tp", axis=0, tiled=True)
    grad_flat = jnp.dot(full_rows, w_out, preferred_element_type=jnp.float32).astype(jnp.bfloat16)
    grad_tiles = grad_flat.reshape(local_tiles, tile_len, col_width)
    head_parts = to_head((k_act, v_act, q_act), local_tiles, tile_len, heads_here)
    key_h = head_parts[:, 0]
    value_h = head_parts[:, 1]
    query_h = head_parts[:, 2]
    grad_h = to_head((grad_tiles,), local_tiles, tile_len, heads_here)[:, 0]
    kv_all = ring_gather(head_parts[:, 0:2], "z", z_count)
    near_index = ring_index(near_slots.reshape(-1), own_z, chip_tiles, z_count)
    near = kv_all[near_index].reshape(chip_tiles, list_len, 2, tile_len, HD)
    near_keys = near[:, :, 0].reshape(chip_tiles, list_len * tile_len, HD)
    near_values = near[:, :, 1].reshape(chip_tiles, list_len * tile_len, HD)
    live_cells = jnp.repeat(near_live > 0, tile_len, axis=1)[:, None, :]
    scores = (
        jnp.einsum("sad,sbd->sab", query_h, near_keys, preferred_element_type=jnp.float32)
        * score_scale
    )
    row_peak = jnp.max(jnp.where(live_cells, scores, -1e30), axis=2, keepdims=True)
    row_total = jnp.sum(
        jnp.where(live_cells, jnp.exp(scores - row_peak), 0.0), axis=2, keepdims=True
    )
    log_total = row_peak + jnp.log(row_total)
    prob_full = jnp.where(live_cells, jnp.exp(scores - log_total), 0.0)
    prob_half = prob_full.astype(jnp.bfloat16)
    attn_h = jnp.einsum(
        "sab,sbd->sad", prob_half, near_values, preferred_element_type=jnp.float32
    ).astype(jnp.bfloat16)
    row_delta = jnp.einsum("sad,sad->sa", grad_h, attn_h, preferred_element_type=jnp.float32)
    grad_prob = jnp.einsum("sad,sbd->sab", grad_h, near_values, preferred_element_type=jnp.float32)
    grad_score = (prob_full * (grad_prob - row_delta[:, :, None])).astype(jnp.bfloat16)
    grad_query_h = (
        jnp.einsum("sab,sbd->sad", grad_score, near_keys, preferred_element_type=jnp.float32)
        * score_scale
    ).astype(jnp.bfloat16)
    attn_tiles, grad_q = from_head((attn_h, grad_query_h), local_tiles, tile_len, heads_here)
    qg_all = lax.all_gather(jnp.stack([query_h, grad_h], axis=1), "z", axis=0, tiled=True)
    stats_all = lax.all_gather(
        jnp.stack([log_total[:, :, 0], row_delta], axis=1), "z", axis=0, tiled=True
    )
    owned_slots = first_slot + jnp.arange(chip_tiles, dtype=jnp.int32)
    pair_hits = (key_slot[:, :, None] == owned_slots[None, None, :]) & (live_mask[:, :, None] > 0)
    named_by = jnp.any(pair_hits, axis=1).astype(jnp.int32)
    rank_of = jnp.cumsum(named_by, axis=0) - 1
    list_pos = jnp.arange(list_len, dtype=jnp.int32)
    placed = (named_by[:, :, None] > 0) & (rank_of[:, :, None] == list_pos[None, None, :])
    slot_index = jnp.arange(tile_count, dtype=jnp.int32)
    picked = jnp.sum(placed.astype(jnp.int32) * slot_index[:, None, None], axis=0)
    picked_live = jnp.any(placed, axis=0)
    picked_index = picked.reshape(-1)
    rows = qg_all[picked_index].reshape(chip_tiles, list_len, 2, tile_len, HD)
    query_rows = rows[:, :, 0].reshape(chip_tiles, list_len * tile_len, HD)
    grad_rows = rows[:, :, 1].reshape(chip_tiles, list_len * tile_len, HD)
    stat_rows = stats_all[picked_index].reshape(chip_tiles, list_len, 2, tile_len)
    total_rows = stat_rows[:, :, 0].reshape(chip_tiles, 1, list_len * tile_len)
    delta_rows = stat_rows[:, :, 1].reshape(chip_tiles, 1, list_len * tile_len)
    keep_pair = jnp.repeat(picked_live, tile_len, axis=1)[:, None, :]
    owner_scores = (
        jnp.einsum("tbd,tad->tba", key_h, query_rows, preferred_element_type=jnp.float32)
        * score_scale
    )
    owner_probs = jnp.where(keep_pair, jnp.exp(owner_scores - total_rows), 0.0)
    owner_grad_prob = jnp.einsum(
        "tbd,tad->tba", value_h, grad_rows, preferred_element_type=jnp.float32
    )
    owner_grad_score = (owner_probs * (owner_grad_prob - delta_rows)).astype(jnp.bfloat16)
    grad_key_h = (
        jnp.einsum("tba,tad->tbd", owner_grad_score, query_rows, preferred_element_type=jnp.float32)
        * score_scale
    ).astype(jnp.bfloat16)
    grad_value_h = jnp.einsum(
        "tba,tad->tbd",
        owner_probs.astype(jnp.bfloat16),
        grad_rows,
        preferred_element_type=jnp.float32,
    ).astype(jnp.bfloat16)
    grad_k, grad_v = from_head((grad_key_h, grad_value_h), local_tiles, tile_len, heads_here)
    attn_flat = attn_tiles.reshape(local_tiles * tile_len, col_width)
    weight_part = lax.dot_general(
        full_rows, attn_flat, (((0,), (0,)), ((), ())), preferred_element_type=jnp.float32
    )
    model_width = weight_part.shape[0]
    block_rows = model_width // (z_count * CORES)
    by_core = weight_part.reshape(z_count, CORES, block_rows, col_width).transpose(1, 0, 2, 3)
    chip_sum = lax.psum_scatter(by_core, "core", scatter_dimension=0, tiled=True)
    grad_weight = lax.psum_scatter(
        chip_sum.reshape(z_count * block_rows, col_width).astype(jnp.bfloat16),
        "z",
        scatter_dimension=0,
        tiled=True,
    )
    return (grad_q, grad_k, grad_v, grad_weight)


def solution(mesh):
    ctx_count = mesh.shape["ctx"]
    tp_count = mesh.shape["tp"]
    devices = mesh.devices.reshape(ctx_count // CORES, CORES, tp_count)
    chip_mesh = Mesh(devices, ("z", "core", "tp"))
    tiles = ("z", "core")
    in_specs = (
        P(tiles, None, "tp"),
        P(tiles, None, "tp"),
        P(tiles, None, "tp"),
        P((*tiles, "tp"), None),
        P(None, "tp"),
        P(),
        P(),
        P(),
    )
    out_specs = (P(tiles, None, "tp"), P(tiles, None, "tp"), P(tiles, None, "tp"), P(tiles, "tp"))
    return jax.shard_map(
        per_device, mesh=chip_mesh, in_specs=in_specs, out_specs=out_specs, check_vma=False
    )
```

profile of v0, /device:TPU:4, one launch (start us, length us, event | category | flops | bytes accessed | tf_op | source)
XLA Modules:
  0.0 305.9 jit_solution(6664586194276471653)
XLA Ops:
  10.2 1.8 copy.60
  14.2 5.4 %all_to_all.66 = bf16[4,3,128,2,128]{4,2,0,1,3:T(8,128)(2,1)S(1)} all-to-all(bf16[4,3,128,2,128]{4,2,0,1,3:T(8,128)(2,1)} %copy.63), channel_id=1, replica_groups=mesh['z'=8,'core'=2,'tp'=16] {'core'}, dimensions={3} | all-to-all | bytes 1572864 | tf_op jit(solution)/shard_map/all_to_all | solution.py:25
  19.8 50.1 %all-gather.3.cloned.1.call-done = bf16[512,4096]{1,0:T(8,128)(2,1)} async-done(((bf16[32,4096]{1,0:T(8,128)(2,1)}), bf16[512,4096]{1,0:T(8,128)(2,1)}) %all-gather.3.cloned.1.call-update) | async-done | bytes 4194320 | tf_op jit(solution)/shard_map/all_gather | solution.py:75
  69.8 3.4 %convolution_convert_fusion = bf16[512,256]{1,0:T(8,128)(2,1)S(1)} fusion(bf16[512,4096]{1,0:T(8,128)(2,1)} %all-gather.3.cloned.1.call-done, bf16[4096,256]{1,0:T(8,128)(2,1)S(1)} %copy-done), kind=kOutput, calls=%fused_computation.29 | convolution fusion | flops 1073872896 | bytes 6553600 | tf_op jit(solution)/shard_map/dot_general | solution.py:76
  73.4 3.9 %all_to_all.67 = bf16[4,1,128,2,128]{4,2,0,1,3:T(8,128)(2,1)S(1)} all-to-all(bf16[4,1,128,2,128]{4,2,0,1,3:T(8,128)(2,1)S(1)} %copy.67), channel_id=1, replica_groups=mesh['z'=8,'core'=2,'tp'=16] {'core'}, dimensions={3} | all-to-all | bytes 524288 | tf_op jit(solution)/shard_map/all_to_all | solution.py:25
  79.3 3.3 %collective-permute-start = (bf16[8,2,128,128]{3,2,0,1:T(8,128)(2,1)S(1)}, bf16[8,2,128,128]{3,2,0,1:T(8,128)(2,1)S(1)}, u32[]{:S(2)}, u32[]{:S(2)}) collective-permute-start(bf16[8,2,128,128]{3,2,0,1:T(8,128)(2,1)S(1)} %get-tuple-element.10), channel_id=1, source_target_pairs={{0,224},{32,0},{64,32},{96,64},{128,96},{160,128},{192,160},{224,1... | collective-permute-start | bytes 1572872 | tf_op jit(solution)/shard_map/ppermute | solution.py:46
  83.5 16.3 %collective-permute-done = bf16[8,2,128,128]{3,2,0,1:T(8,128)(2,1)S(1)} collective-permute-done((bf16[8,2,128,128]{3,2,0,1:T(8,128)(2,1)S(1)}, bf16[8,2,128,128]{3,2,0,1:T(8,128)(2,1)S(1)}, u32[]{:S(2)}, u32[]{:S(2)}) %collective-permute-start) | collective-permute-done | bytes 524320 | tf_op jit(solution)/shard_map/ppermute | solution.py:46
  99.8 3.7 %collective-permute-start.1 = (bf16[8,2,128,128]{3,2,0,1:T(8,128)(2,1)S(1)}, bf16[8,2,128,128]{3,2,0,1:T(8,128)(2,1)S(1)}, u32[]{:S(2)}, u32[]{:S(2)}) collective-permute-start(bf16[8,2,128,128]{3,2,0,1:T(8,128)(2,1)S(1)} %collective-permute-done), channel_id=1, source_target_pairs={{0,224},{32,0},{64,32},{96,64},{128,96},{160,128},{192,160},{224,1... | collective-permute-start | bytes 1572872 | tf_op jit(solution)/shard_map/ppermute | solution.py:46
  103.8 25.9 %collective-permute-done.4 = bf16[8,2,128,128]{3,2,0,1:T(8,128)(2,1)S(1)} collective-permute-done((bf16[8,2,128,128]{3,2,0,1:T(8,128)(2,1)S(1)}, bf16[8,2,128,128]{3,2,0,1:T(8,128)(2,1)S(1)}, u32[]{:S(2)}, u32[]{:S(2)}) %collective-permute-start.4) | collective-permute-done | bytes 524320 | tf_op jit(solution)/shard_map/ppermute | solution.py:47
  129.7 3.3 %collective-permute-start.2 = (bf16[8,2,128,128]{3,2,0,1:T(8,128)(2,1)S(1)}, bf16[8,2,128,128]{3,2,0,1:T(8,128)(2,1)S(1)}, u32[]{:S(2)}, u32[]{:S(2)}) collective-permute-start(bf16[8,2,128,128]{3,2,0,1:T(8,128)(2,1)S(1)} %collective-permute-done.1), channel_id=1, source_target_pairs={{0,224},{32,0},{64,32},{96,64},{128,96},{160,128},{192,160},{224,1... | collective-permute-start | bytes 1572872 | tf_op jit(solution)/shard_map/ppermute | solution.py:46
  133.1 22.4 %collective-permute-done.5 = bf16[8,2,128,128]{3,2,0,1:T(8,128)(2,1)S(1)} collective-permute-done((bf16[8,2,128,128]{3,2,0,1:T(8,128)(2,1)S(1)}, bf16[8,2,128,128]{3,2,0,1:T(8,128)(2,1)S(1)}, u32[]{:S(2)}, u32[]{:S(2)}) %collective-permute-start.5) | collective-permute-done | bytes 524320 | tf_op jit(solution)/shard_map/ppermute | solution.py:47
  155.7 1.9 constant_dynamic-update-slice_fusion.7
  157.6 3.5 %collective-permute-start.7 = (bf16[4,2,128,128]{3,2,0,1:T(8,128)(2,1)S(1)}, bf16[4,2,128,128]{3,2,0,1:T(8,128)(2,1)S(1)}, u32[]{:S(2)}, u32[]{:S(2)}) collective-permute-start(bf16[4,2,128,128]{3,2,0,1:T(8,128)(2,1)S(1)} %slice.73), channel_id=1, source_target_pairs={{0,224},{32,0},{64,32},{96,64},{128,96},{160,128},{192,160},{224,1... | collective-permute-start | bytes 786440 | tf_op jit(solution)/shard_map/ppermute | solution.py:53
  162.9 2.0 collective-permute-done.6
  169.1 8.2 %gather_fusion = bf16[96,2,128,128]{3,2,1,0:T(8,128)(2,1)} fusion(bf16[64,2,128,128]{3,2,0,1:T(8,128)(2,1)} %constant_dynamic-update-slice_fusion, s32[1024]{0:T(1024)S(1)} %pad_clamp_fusion.1), kind=kCustom, calls=%fused_computation | custom fusion | bytes 12583296 | tf_op jit(solution)/shard_map/gather | solution.py:85
  177.3 4.2 %fusion.58 = (bf16[8,12,1,128,128]{4,3,2,1,0:T(8,128)(2,1)S(1)}, bf16[8,12,1,128,128]{4,3,2,1,0:T(8,128)(2,1)S(1)}) fusion(bf16[8,12,2,128,128]{4,3,2,1,0:T(8,128)(2,1)} %bitcast.106), kind=kLoop, calls=%fused_computation.110 | loop fusion | bytes 12582912 | tf_op jit(solution)/shard_map/slice | solution.py:87
  183.2 1.5 select_reduce_fusion
  184.7 1.7 fusion.31
  186.4 7.4 %fusion.27 = bf16[8,1,128,128]{3,2,0,1:T(8,128)(2,1)S(1)} fusion(bf16[8,1536,128]{2,1,0:T(8,128)(2,1)} %bitcast.112, f32[8,128,1536]{2,1,0:T(8,128)} %copy-done.2, bf16[8,128,128]{2,1,0:T(8,128)(2,1)S(1)} %bitcast.129, bf16[8,1536,128]{2,1,0:T(8,128)(2,1)} %bitcast.123, f32[8,128]{1,0:T(8,128)S(1)} %get-tuple-element.20, f32[8,128]{1,0:T(8,128)S(1)} %log_add_fusion, ...), kind=kOutput, calls=%fused_computation.32 | convolution fusion | flops 815005696 | bytes 13127680 | tf_op jit(solution)/shard_map/sab,sbd->sad/dot_general | solution.py:107
  193.9 4.4 %all_to_all.68 = bf16[8,2,128,1,128]{4,2,1,3,0:T(8,128)(2,1)S(1)} all-to-all(bf16[8,2,128,1,128]{4,2,1,3,0:T(8,128)(2,1)S(1)} %copy.68), channel_id=1, replica_groups=mesh['z'=8,'core'=2,'tp'=16] {'core'}, dimensions={0} | all-to-all | bytes 1048576 | tf_op jit(solution)/shard_map/all_to_all | solution.py:31
  199.2 3.4 %convolution_bitcast_fusion = f32[4096,256]{0,1:T(8,128)} fusion(bf16[512,4096]{1,0:T(8,128)(2,1)S(1)} %copy-done.4, bf16[64,8,2,128]{3,2,1,0:T(2,128)(2,1)S(1)} %bitcast.127), kind=kOutput, calls=%fused_computation.9 | convolution fusion | flops 1073741824 | bytes 8650752 | tf_op jit(solution)/shard_map/dot_general | solution.py:153
  202.6 6.6 %reshape.268 = f32[8,2,256,256]{2,1,0,3:T(2,128)} reshape(f32[4096,256]{0,1:T(8,128)} %convolution_bitcast_fusion) | data formatting | bytes 8388608 | tf_op jit(solution)/shard_map/reshape | solution.py:158
  209.2 7.2 %copy.76 = f32[8,2,256,256]{3,2,0,1:T(8,128)} copy(f32[8,2,256,256]{2,1,0,3:T(2,128)} %reshape.268) | data formatting | bytes 8388608 | tf_op jit(solution)/shard_map/reshape | solution.py:158
  218.6 24.6 %all_gather.11 = f32[64,2,128]{2,1,0:T(2,128)S(1)} all-gather(f32[8,2,128]{2,1,0:T(2,128)S(1)} %pad_maximum_fusion.2), channel_id=1, replica_groups=mesh['z'=8,'core'=2,'tp'=16] {'z'}, dimensions={0}, use_global_device_ids=true | all-gather | bytes 73728 | tf_op jit(solution)/shard_map/all_gather | solution.py:112
  244.2 8.2 %gather_fusion.1 = bf16[96,2,128,128]{3,2,1,0:T(8,128)(2,1)} fusion(bf16[64,2,128,128]{3,2,0,1:T(8,128)(2,1)} %all-gather.5.cloned.1.call-done, s32[1024]{0:T(1024)S(1)} %pad_clamp_fusion), kind=kCustom, calls=%fused_computation.1 | custom fusion | bytes 12583296 | tf_op jit(solution)/shard_map/gather | solution.py:125
  252.4 8.1 %fusion.57 = (bf16[8,12,1,128,128]{4,3,2,1,0:T(8,128)(2,1)}, bf16[8,12,1,128,128]{4,3,2,1,0:T(8,128)(2,1)}) fusion(bf16[8,12,2,128,128]{4,3,2,1,0:T(8,128)(2,1)} %bitcast.107), kind=kLoop, calls=%fused_computation.109 | loop fusion | bytes 12582912 | tf_op jit(solution)/shard_map/slice | solution.py:126
  260.5 2.7 convert_element_type.57
  263.2 3.0 fusion.34
  267.6 1.3 copy-done.5
  268.9 7.6 %fusion.26 = bf16[8,1,128,128]{3,2,0,1:T(8,128)(2,1)S(1)} fusion(bf16[8,1536,128]{2,1,0:T(8,128)(2,1)} %bitcast.110, f32[8,128,1536]{2,1,0:T(8,128)} %copy-done.5, bf16[8,1536,128]{2,1,0:T(8,128)(2,1)} %bitcast.120, f32[8,1536]{1,0:T(8,128)S(1)} %get-tuple-element.24, f32[8,1536]{1,0:T(8,128)S(1)} %get-tuple-element.25, ...), kind=kOutput, calls=%fused_computation.31 | convolution fusion | flops 815005696 | bytes 13217792 | tf_op jit(solution)/shard_map/tba,tad->tbd/dot_general | solution.py:142
  276.6 4.2 %all_to_all.69 = bf16[8,2,128,1,128]{4,2,1,3,0:T(8,128)(2,1)S(1)} all-to-all(bf16[8,2,128,1,128]{4,2,1,3,0:T(8,128)(2,1)S(1)} %copy.73), channel_id=1, replica_groups=mesh['z'=8,'core'=2,'tp'=16] {'core'}, dimensions={0} | all-to-all | bytes 1048576 | tf_op jit(solution)/shard_map/all_to_all | solution.py:31
  283.1 16.3 %reduce-scatter.5.cloned.1.call-done = bf16[256,256]{1,0:T(8,128)(2,1)} async-done(((bf16[2048,256]{1,0:T(8,128)(2,1)}), bf16[256,256]{1,0:T(8,128)(2,1)}) %reduce-scatter.5.cloned.1.call-update) | async-done | bytes 131088 | tf_op jit(solution)/shard_map/reduce_scatter | solution.py:160
  (103 shorter events, 24.3 us)
Async XLA Ops:
  7.2 62.6 %copy-start = (bf16[4096,256]{1,0:T(8,128)(2,1)S(1)}, bf16[4096,256]{1,0:T(8,128)(2,1)}, u32[]{:S(2)}) copy-start(bf16[4096,256]{1,0:T(8,128)(2,1)} %param.12) | copy-start | bytes 6291460
  7.2 62.6 %all-gather.3.cloned.1.call-start = ((), (), s32[]{:S(2)}) async-start(), calls=%async_computation.6 | async-start | bytes 4456448 | tf_op jit(solution)/shard_map/all_gather | solution.py:75
  7.9 236.3 %all-gather.5.cloned.1.call-start = ((), (), s32[]{:S(2)}) async-start(), calls=%async_computation.7 | async-start | bytes 4718592 | tf_op jit(solution)/shard_map/all_gather | solution.py:111
  73.2 9.4 %copy-start.9 = (s32[64]{0:T(128)S(1)}, s32[64]{0:T(128)}, u32[]{:S(2)}) copy-start(s32[64]{0:T(128)} %param.15) | copy-start | bytes 772
  73.3 9.4 %copy-start.10 = (s32[64,12]{0,1:T(8,128)S(1)}, s32[64,12]{0,1:T(8,128)}, u32[]{:S(2)}) copy-start(s32[64,12]{0,1:T(8,128)} %param.13) | copy-start | bytes 9220
  73.3 30.3 %copy-start.11 = (s32[64,12]{0,1:T(8,128)S(1)}, s32[64,12]{0,1:T(8,128)}, u32[]{:S(2)}) copy-start(s32[64,12]{0,1:T(8,128)} %param.14) | copy-start | bytes 9220
  78.2 182.3 %reduce-scatter.3.cloned.1.call-start = ((), (), s32[]{:S(2)}) async-start(), calls=%async_computation.8 | async-start | bytes 6291456 | tf_op jit(solution)/shard_map/reduce_scatter | solution.py:159
  79.3 20.5 %collective-permute-start = (bf16[8,2,128,128]{3,2,0,1:T(8,128)(2,1)S(1)}, bf16[8,2,128,128]{3,2,0,1:T(8,128)(2,1)S(1)}, u32[]{:S(2)}, u32[]{:S(2)}) collective-permute-start(bf16[8,2,128,128]{3,2,0,1:T(8,128)(2,1)S(1)} %get-tuple-element.10), channel_id=1, source_target_pairs={{0,224},{32,0},{64,32},{96,64},{128,96},{160,128},{192,160},{224,1... | collective-permute-start | bytes 1572872 | tf_op jit(solution)/shard_map/ppermute | solution.py:46
  82.6 20.9 %collective-permute-start.3 = (bf16[8,2,128,128]{3,2,0,1:T(8,128)(2,1)S(1)}, bf16[8,2,128,128]{3,2,0,1:T(8,128)(2,1)S(1)}, u32[]{:S(2)}, u32[]{:S(2)}) collective-permute-start(bf16[8,2,128,128]{3,2,0,1:T(8,128)(2,1)S(1)} %get-tuple-element.10), channel_id=1, source_target_pairs={{0,32},{32,64},{64,96},{96,128},{128,160},{160,192},{192,224},{224... | collective-permute-start | bytes 1572872 | tf_op jit(solution)/shard_map/ppermute | solution.py:47
  99.8 29.9 %copy-start.8 = (bf16[8,2,128,128]{3,2,0,1:T(8,128)(2,1)}, bf16[8,2,128,128]{3,2,0,1:T(8,128)(2,1)S(1)}, u32[]{:S(2)}) copy-start(bf16[8,2,128,128]{3,2,0,1:T(8,128)(2,1)S(1)} %collective-permute-done) | copy-start | bytes 1572868
  99.8 29.9 %collective-permute-start.1 = (bf16[8,2,128,128]{3,2,0,1:T(8,128)(2,1)S(1)}, bf16[8,2,128,128]{3,2,0,1:T(8,128)(2,1)S(1)}, u32[]{:S(2)}, u32[]{:S(2)}) collective-permute-start(bf16[8,2,128,128]{3,2,0,1:T(8,128)(2,1)S(1)} %collective-permute-done), channel_id=1, source_target_pairs={{0,224},{32,0},{64,32},{96,64},{128,96},{160,128},{192,160},{224,1... | collective-permute-start | bytes 1572872 | tf_op jit(solution)/shard_map/ppermute | solution.py:46
  103.5 26.1 %collective-permute-start.4 = (bf16[8,2,128,128]{3,2,0,1:T(8,128)(2,1)S(1)}, bf16[8,2,128,128]{3,2,0,1:T(8,128)(2,1)S(1)}, u32[]{:S(2)}, u32[]{:S(2)}) collective-permute-start(bf16[8,2,128,128]{3,2,0,1:T(8,128)(2,1)S(1)} %collective-permute-done.3), channel_id=1, source_target_pairs={{0,32},{32,64},{64,96},{96,128},{128,160},{160,192},{192,224},{224... | collective-permute-start | bytes 1572872 | tf_op jit(solution)/shard_map/ppermute | solution.py:47
  129.7 25.9 %collective-permute-start.5 = (bf16[8,2,128,128]{3,2,0,1:T(8,128)(2,1)S(1)}, bf16[8,2,128,128]{3,2,0,1:T(8,128)(2,1)S(1)}, u32[]{:S(2)}, u32[]{:S(2)}) collective-permute-start(bf16[8,2,128,128]{3,2,0,1:T(8,128)(2,1)S(1)} %collective-permute-done.4), channel_id=1, source_target_pairs={{0,32},{32,64},{64,96},{96,128},{128,160},{160,192},{192,224},{224... | collective-permute-start | bytes 1572872 | tf_op jit(solution)/shard_map/ppermute | solution.py:47
  129.7 27.9 %collective-permute-start.2 = (bf16[8,2,128,128]{3,2,0,1:T(8,128)(2,1)S(1)}, bf16[8,2,128,128]{3,2,0,1:T(8,128)(2,1)S(1)}, u32[]{:S(2)}, u32[]{:S(2)}) collective-permute-start(bf16[8,2,128,128]{3,2,0,1:T(8,128)(2,1)S(1)} %collective-permute-done.1), channel_id=1, source_target_pairs={{0,224},{32,0},{64,32},{96,64},{128,96},{160,128},{192,160},{224,1... | collective-permute-start | bytes 1572872 | tf_op jit(solution)/shard_map/ppermute | solution.py:46
  155.6 9.4 %collective-permute-start.6 = (bf16[4,2,128,128]{3,2,0,1:T(8,128)(2,1)S(1)}, bf16[4,2,128,128]{3,2,0,1:T(8,128)(2,1)S(1)}, u32[]{:S(2)}, u32[]{:S(2)}) collective-permute-start(bf16[4,2,128,128]{3,2,0,1:T(8,128)(2,1)S(1)} %slice.72), channel_id=1, source_target_pairs={{0,32},{32,64},{64,96},{96,128},{128,160},{160,192},{192,224},{224... | collective-permute-start | bytes 786440 | tf_op jit(solution)/shard_map/ppermute | solution.py:52
  157.6 8.1 %collective-permute-start.7 = (bf16[4,2,128,128]{3,2,0,1:T(8,128)(2,1)S(1)}, bf16[4,2,128,128]{3,2,0,1:T(8,128)(2,1)S(1)}, u32[]{:S(2)}, u32[]{:S(2)}) collective-permute-start(bf16[4,2,128,128]{3,2,0,1:T(8,128)(2,1)S(1)} %slice.73), channel_id=1, source_target_pairs={{0,224},{32,0},{64,32},{96,64},{128,96},{160,128},{192,160},{224,1... | collective-permute-start | bytes 786440 | tf_op jit(solution)/shard_map/ppermute | solution.py:53
  181.6 1.6 copy-start.3
  181.6 3.1 %copy-start.7 = (bf16[8,12,1,128,128]{4,3,2,1,0:T(8,128)(2,1)}, bf16[8,12,1,128,128]{4,3,2,1,0:T(8,128)(2,1)S(1)}, u32[]{:S(2)}) copy-start(bf16[8,12,1,128,128]{4,3,2,1,0:T(8,128)(2,1)S(1)} %get-tuple-element.8) | copy-start | bytes 9437188
  183.2 3.2 %copy-start.2 = (f32[8,128,1536]{2,1,0:T(8,128)}, f32[8,128,1536]{2,1,0:T(8,128)S(1)}, u32[]{:S(2)}) copy-start(f32[8,128,1536]{2,1,0:T(8,128)S(1)} %get-tuple-element.19) | copy-start | bytes 18874372
  193.8 5.5 %copy-start.4 = (bf16[512,4096]{1,0:T(8,128)(2,1)S(1)}, bf16[512,4096]{1,0:T(8,128)(2,1)}, u32[]{:S(2)}) copy-start(bf16[512,4096]{1,0:T(8,128)(2,1)} %all-gather.3.cloned.1.call-done) | copy-start | bytes 12582916
  216.5 82.9 %reduce-scatter.5.cloned.1.call-start = ((), (), s32[]{:S(2)}) async-start(), calls=%async_computation.9 | async-start | bytes 1179648 | tf_op jit(solution)/shard_map/reduce_scatter | solution.py:160
  263.2 3.0 copy-start.6
  266.2 2.7 copy-start.5
  268.9 30.5 %copy-start.1 = (bf16[4096,256]{1,0:T(8,128)(2,1)S(1)}, bf16[4096,256]{1,0:T(8,128)(2,1)}, u32[]{:S(2)}) copy-start(bf16[4096,256]{1,0:T(8,128)(2,1)} %param.12) | copy-start | bytes 6291460
Sparse Core Ops, SparseCore 0:
  10.4 59.3 all-gather.2
  78.3 83.5 all-gather.4
  216.6 14.3 reduce-scatter.2
  263.3 35.9 reduce-scatter.4
where the time goes:
time: 307 us; the launch traced here: 306 us
  waiting for transfers between devices  134 us (44%)
  local copies, waits for them, and re-layouts  64.6 us (21%)
  blocking collectives  42.6 us (14%)
  matrix products  29.3 us (10%)
  between operations  14.2 us (5%)
  starting transfers between devices  14 us (5%)
  other arithmetic  7.47 us (2%)
    all_gather x1, waiting for transfers between devices, per_device(): full_rows = lax.all_gather(grad_out, 'tp', axis=0, tiled=True)  50.1 us
    ppermute x3, waiting for transfers between devices, ring_gather(): up = lax.ppermute(up, axis, behind)  48.3 us
    all_gather x1, blocking collectives, per_device(): lax.all_gather(jnp.stack([log_total[:, :, 0], row_delta], axis=1), 'z', a...  24.6 us
    ppermute x3, waiting for transfers between devices, ring_gather(): down = lax.ppermute(down, axis, ahead)  16.3 us
    reduce_scatter x1, waiting for transfers between devices, per_device(): lax.psum_scatter(chip_sum.reshape(z_count * block_rows, col_width).astype...  16.3 us
    reshape x2, local copies, waits for them, and re-layouts, per_device(): weight_part.reshape(z_count, CORES, block_rows, col_width)  13.8 us
    unnamed x34, local copies, waits for them, and re-layouts  12.9 us
    ppermute x3, starting transfers between devices, ring_gather(): down = lax.ppermute(down, axis, ahead)  10.3 us
  transfers between devices with their start and end apart: 12, of which 6 were waited for; matrix products, arithmetic and copies ran while one was open for 30% of the time, Pallas kernels for 0%

commit v1 on v0

--- a/solution.py
+++ b/solution.py
@@ -72,7 +72,9 @@
     list_len = key_slot.shape[1]
     near_slots = lax.dynamic_slice_in_dim(key_slot, first_slot, chip_tiles, 0)
     near_live = lax.dynamic_slice_in_dim(live_mask, first_slot, chip_tiles, 0)
-    full_rows = lax.all_gather(grad_out, "tp", axis=0, tiled=True)
+    full_rows = jnp.concatenate(
+        lax.all_to_all(jnp.stack([grad_out] * lax.axis_size("tp")), "tp", 0, 0), axis=0
+    )
     grad_flat = jnp.dot(full_rows, w_out, preferred_element_type=jnp.float32).astype(jnp.bfloat16)
     grad_tiles = grad_flat.reshape(local_tiles, tile_len, col_width)
     head_parts = to_head((k_act, v_act, q_act), local_tiles, tile_len, heads_here)

time: 307 us -> 341 us (1.11)
  waiting for transfers between devices: 134 us -> 149 us
  starting transfers between devices: 14 us -> 24 us
  local copies, waits for them, and re-layouts: 64.6 us -> 69.5 us
    all_to_all x0 -> x1, waiting for transfers between devices: none -> 59.4 us  [per_device(): lax.all_to_all(jnp.stack([grad_out] * lax.axis_size('tp')), 'tp', 0, 0)]
    all_gather x1 -> x0, waiting for transfers between devices: 50.1 us -> none  [per_device(): full_rows = lax.all_gather(grad_out, 'tp', axis=0, tiled=True)]
    all_to_all x0 -> x1, starting transfers between devices: none -> 7.45 us  [per_device(): lax.all_to_all(jnp.stack([grad_out] * lax.axis_size('tp')), 'tp', 0, 0)]
    ppermute x3, waiting for transfers between devices: 16.3 us -> 10.6 us  [ring_gather(): down = lax.ppermute(down, axis, ahead)]
    reduce_scatter x1, waiting for transfers between devices: 16.3 us -> 21.9 us  [per_device(): lax.psum_scatter(chip_sum.reshape(z_count * block_rows, col_width).astype...]
    ppermute x1, waiting for transfers between devices: 2.02 us -> 7.42 us  [ring_gather(): first = lax.ppermute(up[:cut], axis, behind)]
    unnamed x34 -> x32, local copies, waits for them, and re-layouts: 12.9 us -> 13.1 us
  transfers between devices with their start and end apart: 12 -> 12, of which waited for: 6 -> 6; matrix products, arithmetic and copies ran while one was open for 30% -> 26% of each run, Pallas kernels for 0% -> 0%
where the time goes in v1:
time: 341 us; the launch traced here: 340 us
  waiting for transfers between devices  149 us (44%)
  local copies, waits for them, and re-layouts  69.5 us (20%)
  blocking collectives  43.2 us (13%)
  matrix products  31.3 us (9%)
  starting transfers between devices  24 us (7%)
  between operations  15.9 us (5%)
  other arithmetic  7.47 us (2%)
    all_to_all x1, waiting for transfers between devices, per_device(): lax.all_to_all(jnp.stack([grad_out] * lax.axis_size('tp')), 'tp', 0, 0)  59.4 us
    ppermute x3, waiting for transfers between devices, ring_gather(): up = lax.ppermute(up, axis, behind)  49.3 us
    all_gather x1, blocking collectives, per_device(): lax.all_gather(jnp.stack([log_total[:, :, 0], row_delta], axis=1), 'z', a...  24.6 us
    reduce_scatter x1, waiting for transfers between devices, per_device(): lax.psum_scatter(chip_sum.reshape(z_count * block_rows, col_width).astype...  21.9 us
    reshape x2, local copies, waits for them, and re-layouts, per_device(): weight_part.reshape(z_count, CORES, block_rows, col_width)  13.8 us
    unnamed x32, local copies, waits for them, and re-layouts  13.1 us
    ppermute x3, starting transfers between devices, ring_gather(): down = lax.ppermute(down, axis, ahead)  12.9 us
    ppermute x3, waiting for transfers between devices, ring_gather(): down = lax.ppermute(down, axis, ahead)  10.6 us
  transfers between devices with their start and end apart: 12, of which 6 were waited for; matrix products, arithmetic and copies ran while one was open for 26% of the time, Pallas kernels for 0%

profile of v1, /device:TPU:4, one launch (start us, length us, event | category | flops | bytes accessed | tf_op | source)
XLA Modules:
  0.0 339.9 jit_solution(13576622672115894553)
XLA Ops:
  10.4 1.8 copy.60
  14.4 6.3 %all_to_all.71 = bf16[4,3,128,2,128]{4,2,0,1,3:T(8,128)(2,1)} all-to-all(bf16[4,3,128,2,128]{4,2,0,1,3:T(8,128)(2,1)} %copy.63), channel_id=1, replica_groups=mesh['z'=8,'core'=2,'tp'=16] {'core'}, dimensions={3} | all-to-all | bytes 1572864 | tf_op jit(solution)/shard_map/all_to_all | solution.py:25
  20.8 3.4 stack.24
  24.2 7.5 %all-to-all-start.1 = ((bf16[16,32,4096]{2,1,0:T(8,128)(2,1)}), bf16[16,32,4096]{2,1,0:T(8,128)(2,1)}, u32[]{:S(2)}, u32[]{:S(2)}) async-start(bf16[16,32,4096]{2,1,0:T(8,128)(2,1)} %stack.24), calls=%async_computation.1 | async-start | bytes 8388608 | tf_op jit(solution)/shard_map/all_to_all | solution.py:76
  32.9 59.4 %all-to-all-done.1 = bf16[16,32,4096]{2,1,0:T(8,128)(2,1)} async-done(((bf16[16,32,4096]{2,1,0:T(8,128)(2,1)}), bf16[16,32,4096]{2,1,0:T(8,128)(2,1)}, u32[]{:S(2)}, u32[]{:S(2)}) %all-to-all-start.1) | async-done | bytes 4194336 | tf_op jit(solution)/shard_map/all_to_all | solution.py:76
  92.3 3.4 %convolution_convert_fusion = bf16[512,256]{1,0:T(8,128)(2,1)S(1)} fusion(bf16[512,4096]{1,0:T(8,128)(2,1)} %bitcast.13, bf16[4096,256]{1,0:T(8,128)(2,1)S(1)} %copy-done), kind=kOutput, calls=%fused_computation.29 | convolution fusion | flops 1073872896 | bytes 6553600 | tf_op jit(solution)/shard_map/dot_general | solution.py:78
  95.9 3.9 %all_to_all.72 = bf16[4,1,128,2,128]{4,2,0,1,3:T(8,128)(2,1)S(1)} all-to-all(bf16[4,1,128,2,128]{4,2,0,1,3:T(8,128)(2,1)S(1)} %copy.67), channel_id=1, replica_groups=mesh['z'=8,'core'=2,'tp'=16] {'core'}, dimensions={3} | all-to-all | bytes 524288 | tf_op jit(solution)/shard_map/all_to_all | solution.py:25
  101.8 5.9 %collective-permute-start = (bf16[8,2,128,128]{3,2,0,1:T(8,128)(2,1)S(1)}, bf16[8,2,128,128]{3,2,0,1:T(8,128)(2,1)S(1)}, u32[]{:S(2)}, u32[]{:S(2)}) collective-permute-start(bf16[8,2,128,128]{3,2,0,1:T(8,128)(2,1)S(1)} %get-tuple-element.10), channel_id=1, source_target_pairs={{0,224},{32,0},{64,32},{96,64},{128,96},{160,128},{192,160},{224,1... | collective-permute-start | bytes 1572872 | tf_op jit(solution)/shard_map/ppermute | solution.py:46
  108.6 10.6 %collective-permute-done = bf16[8,2,128,128]{3,2,0,1:T(8,128)(2,1)S(1)} collective-permute-done((bf16[8,2,128,128]{3,2,0,1:T(8,128)(2,1)S(1)}, bf16[8,2,128,128]{3,2,0,1:T(8,128)(2,1)S(1)}, u32[]{:S(2)}, u32[]{:S(2)}) %collective-permute-start) | collective-permute-done | bytes 524320 | tf_op jit(solution)/shard_map/ppermute | solution.py:46
  119.2 3.7 %collective-permute-start.1 = (bf16[8,2,128,128]{3,2,0,1:T(8,128)(2,1)S(1)}, bf16[8,2,128,128]{3,2,0,1:T(8,128)(2,1)S(1)}, u32[]{:S(2)}, u32[]{:S(2)}) collective-permute-start(bf16[8,2,128,128]{3,2,0,1:T(8,128)(2,1)S(1)} %collective-permute-done), channel_id=1, source_target_pairs={{0,224},{32,0},{64,32},{96,64},{128,96},{160,128},{192,160},{224,1... | collective-permute-start | bytes 1572872 | tf_op jit(solution)/shard_map/ppermute | solution.py:46
  123.1 26.4 %collective-permute-done.4 = bf16[8,2,128,128]{3,2,0,1:T(8,128)(2,1)S(1)} collective-permute-done((bf16[8,2,128,128]{3,2,0,1:T(8,128)(2,1)S(1)}, bf16[8,2,128,128]{3,2,0,1:T(8,128)(2,1)S(1)}, u32[]{:S(2)}, u32[]{:S(2)}) %collective-permute-start.4) | collective-permute-done | bytes 524320 | tf_op jit(solution)/shard_map/ppermute | solution.py:47
  149.6 3.3 collective-permute-start.2
  153.0 22.9 %collective-permute-done.5 = bf16[8,2,128,128]{3,2,0,1:T(8,128)(2,1)S(1)} collective-permute-done((bf16[8,2,128,128]{3,2,0,1:T(8,128)(2,1)S(1)}, bf16[8,2,128,128]{3,2,0,1:T(8,128)(2,1)S(1)}, u32[]{:S(2)}, u32[]{:S(2)}) %collective-permute-start.5) | collective-permute-done | bytes 524320 | tf_op jit(solution)/shard_map/ppermute | solution.py:47
  176.0 2.0 constant_dynamic-update-slice_fusion.7
  178.0 3.5 %collective-permute-start.7 = (bf16[4,2,128,128]{3,2,0,1:T(8,128)(2,1)S(1)}, bf16[4,2,128,128]{3,2,0,1:T(8,128)(2,1)S(1)}, u32[]{:S(2)}, u32[]{:S(2)}) collective-permute-start(bf16[4,2,128,128]{3,2,0,1:T(8,128)(2,1)S(1)} %slice.73), channel_id=1, source_target_pairs={{0,224},{32,0},{64,32},{96,64},{128,96},{160,128},{192,160},{224,1... | collective-permute-start | bytes 786440 | tf_op jit(solution)/shard_map/ppermute | solution.py:53
  183.3 7.4 %collective-permute-done.6 = bf16[4,2,128,128]{3,2,0,1:T(8,128)(2,1)S(1)} collective-permute-done((bf16[4,2,128,128]{3,2,0,1:T(8,128)(2,1)S(1)}, bf16[4,2,128,128]{3,2,0,1:T(8,128)(2,1)S(1)}, u32[]{:S(2)}, u32[]{:S(2)}) %collective-permute-start.6) | collective-permute-done | bytes 262176 | tf_op jit(solution)/shard_map/ppermute | solution.py:52
  195.0 8.2 %gather_fusion = bf16[96,2,128,128]{3,2,1,0:T(8,128)(2,1)} fusion(bf16[64,2,128,128]{3,2,0,1:T(8,128)(2,1)} %constant_dynamic-update-slice_fusion, s32[1024]{0:T(1024)S(1)} %pad_clamp_fusion.1), kind=kCustom, calls=%fused_computation | custom fusion | bytes 12583296 | tf_op jit(solution)/shard_map/gather | solution.py:87
  203.2 4.2 %fusion.58 = (bf16[8,12,1,128,128]{4,3,2,1,0:T(8,128)(2,1)S(1)}, bf16[8,12,1,128,128]{4,3,2,1,0:T(8,128)(2,1)S(1)}) fusion(bf16[8,12,2,128,128]{4,3,2,1,0:T(8,128)(2,1)} %bitcast.107), kind=kLoop, calls=%fused_computation.110 | loop fusion | bytes 12582912 | tf_op jit(solution)/shard_map/slice | solution.py:89
  210.5 1.7 fusion.31
  212.2 7.4 %fusion.27 = bf16[8,1,128,128]{3,2,0,1:T(8,128)(2,1)S(1)} fusion(bf16[8,1536,128]{2,1,0:T(8,128)(2,1)} %bitcast.113, f32[8,128,1536]{2,1,0:T(8,128)} %copy-done.2, bf16[8,128,128]{2,1,0:T(8,128)(2,1)S(1)} %bitcast.130, bf16[8,1536,128]{2,1,0:T(8,128)(2,1)} %bitcast.124, f32[8,128]{1,0:T(8,128)S(1)} %get-tuple-element.20, f32[8,128]{1,0:T(8,128)S(1)} %log_add_fusion, ...), kind=kOutput, calls=%fused_computation.32 | convolution fusion | flops 815005696 | bytes 13127680 | tf_op jit(solution)/shard_map/sab,sbd->sad/dot_general | solution.py:109
  219.7 4.2 %all_to_all.73 = bf16[8,2,128,1,128]{4,2,1,3,0:T(8,128)(2,1)S(1)} all-to-all(bf16[8,2,128,1,128]{4,2,1,3,0:T(8,128)(2,1)S(1)} %copy.68), channel_id=1, replica_groups=mesh['z'=8,'core'=2,'tp'=16] {'core'}, dimensions={0} | all-to-all | bytes 1048576 | tf_op jit(solution)/shard_map/all_to_all | solution.py:31
  224.8 5.4 %convolution_bitcast_fusion = f32[4096,256]{0,1:T(8,128)} fusion(bf16[512,4096]{1,0:T(8,128)(2,1)} %bitcast.13, bf16[64,8,2,128]{3,2,1,0:T(2,128)(2,1)S(1)} %bitcast.128), kind=kOutput, calls=%fused_computation.9 | convolution fusion | flops 1073741824 | bytes 8650752 | tf_op jit(solution)/shard_map/dot_general | solution.py:155
  230.2 6.6 %reshape.274 = f32[8,2,256,256]{2,1,0,3:T(2,128)} reshape(f32[4096,256]{0,1:T(8,128)} %convolution_bitcast_fusion) | data formatting | bytes 8388608 | tf_op jit(solution)/shard_map/reshape | solution.py:160
  236.8 7.2 %copy.76 = f32[8,2,256,256]{3,2,0,1:T(8,128)} copy(f32[8,2,256,256]{2,1,0,3:T(2,128)} %reshape.274) | data formatting | bytes 8388608 | tf_op jit(solution)/shard_map/reshape | solution.py:160
  246.2 24.6 %all_gather.7 = f32[64,2,128]{2,1,0:T(2,128)S(1)} all-gather(f32[8,2,128]{2,1,0:T(2,128)S(1)} %pad_maximum_fusion.2), channel_id=1, replica_groups=mesh['z'=8,'core'=2,'tp'=16] {'z'}, dimensions={0}, use_global_device_ids=true | all-gather | bytes 73728 | tf_op jit(solution)/shard_map/all_gather | solution.py:114
  271.9 8.2 %gather_fusion.1 = bf16[96,2,128,128]{3,2,1,0:T(8,128)(2,1)} fusion(bf16[64,2,128,128]{3,2,0,1:T(8,128)(2,1)} %all-gather.2.cloned.1.call-done, s32[1024]{0:T(1024)S(1)} %pad_clamp_fusion), kind=kCustom, calls=%fused_computation.1 | custom fusion | bytes 12583296 | tf_op jit(solution)/shard_map/gather | solution.py:127
  280.0 8.1 %fusion.57 = (bf16[8,12,1,128,128]{4,3,2,1,0:T(8,128)(2,1)}, bf16[8,12,1,128,128]{4,3,2,1,0:T(8,128)(2,1)}) fusion(bf16[8,12,2,128,128]{4,3,2,1,0:T(8,128)(2,1)} %bitcast.108), kind=kLoop, calls=%fused_computation.109 | loop fusion | bytes 12582912 | tf_op jit(solution)/shard_map/slice | solution.py:128
  288.1 2.7 convert_element_type.57
  290.9 3.0 fusion.34
  296.5 7.5 %fusion.26 = bf16[8,1,128,128]{3,2,0,1:T(8,128)(2,1)S(1)} fusion(bf16[8,1536,128]{2,1,0:T(8,128)(2,1)} %bitcast.111, f32[8,128,1536]{2,1,0:T(8,128)} %copy-done.4, bf16[8,1536,128]{2,1,0:T(8,128)(2,1)} %bitcast.121, f32[8,1536]{1,0:T(8,128)S(1)} %get-tuple-element.24, f32[8,1536]{1,0:T(8,128)S(1)} %get-tuple-element.25, ...), kind=kOutput, calls=%fused_computation.31 | convolution fusion | flops 815005696 | bytes 13217792 | tf_op jit(solution)/shard_map/tba,tad->tbd/dot_general | solution.py:144
  304.1 4.2 %all_to_all.74 = bf16[8,2,128,1,128]{4,2,1,3,0:T(8,128)(2,1)S(1)} all-to-all(bf16[8,2,128,1,128]{4,2,1,3,0:T(8,128)(2,1)S(1)} %copy.73), channel_id=1, replica_groups=mesh['z'=8,'core'=2,'tp'=16] {'core'}, dimensions={0} | all-to-all | bytes 1048576 | tf_op jit(solution)/shard_map/all_to_all | solution.py:31
  310.6 21.9 %reduce-scatter.5.cloned.1.call-done = bf16[256,256]{1,0:T(8,128)(2,1)} async-done(((bf16[2048,256]{1,0:T(8,128)(2,1)}), bf16[256,256]{1,0:T(8,128)(2,1)}) %reduce-scatter.5.cloned.1.call-update) | async-done | bytes 131088 | tf_op jit(solution)/shard_map/reduce_scatter | solution.py:162
  (101 shorter events, 27.7 us)
Async XLA Ops:
  8.0 84.3 %copy-start = (bf16[4096,256]{1,0:T(8,128)(2,1)S(1)}, bf16[4096,256]{1,0:T(8,128)(2,1)}, u32[]{:S(2)}) copy-start(bf16[4096,256]{1,0:T(8,128)(2,1)} %param.12) | copy-start | bytes 6291460
  24.2 68.1 %all-to-all-start.1 = ((bf16[16,32,4096]{2,1,0:T(8,128)(2,1)}), bf16[16,32,4096]{2,1,0:T(8,128)(2,1)}, u32[]{:S(2)}, u32[]{:S(2)}) async-start(bf16[16,32,4096]{2,1,0:T(8,128)(2,1)} %stack.24), calls=%async_computation.1 | async-start | bytes 8388608 | tf_op jit(solution)/shard_map/all_to_all | solution.py:76
  31.6 240.2 %all-gather.2.cloned.1.call-start = ((), (), s32[]{:S(2)}) async-start(), calls=%async_computation.7 | async-start | bytes 4718592 | tf_op jit(solution)/shard_map/all_gather | solution.py:113
  95.7 12.0 %copy-start.8 = (s32[64]{0:T(128)S(1)}, s32[64]{0:T(128)}, u32[]{:S(2)}) copy-start(s32[64]{0:T(128)} %param.15) | copy-start | bytes 772
  95.7 11.9 %copy-start.9 = (s32[64,12]{0,1:T(8,128)S(1)}, s32[64,12]{0,1:T(8,128)}, u32[]{:S(2)}) copy-start(s32[64,12]{0,1:T(8,128)} %param.13) | copy-start | bytes 9220
  95.8 27.2 %copy-start.10 = (s32[64,12]{0,1:T(8,128)S(1)}, s32[64,12]{0,1:T(8,128)}, u32[]{:S(2)}) copy-start(s32[64,12]{0,1:T(8,128)} %param.14) | copy-start | bytes 9220
  100.7 187.4 %reduce-scatter.3.cloned.1.call-start = ((), (), s32[]{:S(2)}) async-start(), calls=%async_computation.8 | async-start | bytes 6291456 | tf_op jit(solution)/shard_map/reduce_scatter | solution.py:161
  101.8 17.4 %collective-permute-start = (bf16[8,2,128,128]{3,2,0,1:T(8,128)(2,1)S(1)}, bf16[8,2,128,128]{3,2,0,1:T(8,128)(2,1)S(1)}, u32[]{:S(2)}, u32[]{:S(2)}) collective-permute-start(bf16[8,2,128,128]{3,2,0,1:T(8,128)(2,1)S(1)} %get-tuple-element.10), channel_id=1, source_target_pairs={{0,224},{32,0},{64,32},{96,64},{128,96},{160,128},{192,160},{224,1... | collective-permute-start | bytes 1572872 | tf_op jit(solution)/shard_map/ppermute | solution.py:46
  107.7 15.2 %collective-permute-start.3 = (bf16[8,2,128,128]{3,2,0,1:T(8,128)(2,1)S(1)}, bf16[8,2,128,128]{3,2,0,1:T(8,128)(2,1)S(1)}, u32[]{:S(2)}, u32[]{:S(2)}) collective-permute-start(bf16[8,2,128,128]{3,2,0,1:T(8,128)(2,1)S(1)} %get-tuple-element.10), channel_id=1, source_target_pairs={{0,32},{32,64},{64,96},{96,128},{128,160},{160,192},{192,224},{224... | collective-permute-start | bytes 1572872 | tf_op jit(solution)/shard_map/ppermute | solution.py:47
  119.2 30.4 %copy-start.7 = (bf16[8,2,128,128]{3,2,0,1:T(8,128)(2,1)}, bf16[8,2,128,128]{3,2,0,1:T(8,128)(2,1)S(1)}, u32[]{:S(2)}) copy-start(bf16[8,2,128,128]{3,2,0,1:T(8,128)(2,1)S(1)} %collective-permute-done) | copy-start | bytes 1572868
  119.2 30.4 %collective-permute-start.1 = (bf16[8,2,128,128]{3,2,0,1:T(8,128)(2,1)S(1)}, bf16[8,2,128,128]{3,2,0,1:T(8,128)(2,1)S(1)}, u32[]{:S(2)}, u32[]{:S(2)}) collective-permute-start(bf16[8,2,128,128]{3,2,0,1:T(8,128)(2,1)S(1)} %collective-permute-done), channel_id=1, source_target_pairs={{0,224},{32,0},{64,32},{96,64},{128,96},{160,128},{192,160},{224,1... | collective-permute-start | bytes 1572872 | tf_op jit(solution)/shard_map/ppermute | solution.py:46
  122.9 26.6 %collective-permute-start.4 = (bf16[8,2,128,128]{3,2,0,1:T(8,128)(2,1)S(1)}, bf16[8,2,128,128]{3,2,0,1:T(8,128)(2,1)S(1)}, u32[]{:S(2)}, u32[]{:S(2)}) collective-permute-start(bf16[8,2,128,128]{3,2,0,1:T(8,128)(2,1)S(1)} %collective-permute-done.3), channel_id=1, source_target_pairs={{0,32},{32,64},{64,96},{96,128},{128,160},{160,192},{192,224},{224... | collective-permute-start | bytes 1572872 | tf_op jit(solution)/shard_map/ppermute | solution.py:47
  149.5 26.4 %collective-permute-start.5 = (bf16[8,2,128,128]{3,2,0,1:T(8,128)(2,1)S(1)}, bf16[8,2,128,128]{3,2,0,1:T(8,128)(2,1)S(1)}, u32[]{:S(2)}, u32[]{:S(2)}) collective-permute-start(bf16[8,2,128,128]{3,2,0,1:T(8,128)(2,1)S(1)} %collective-permute-done.4), channel_id=1, source_target_pairs={{0,32},{32,64},{64,96},{96,128},{128,160},{160,192},{192,224},{224... | collective-permute-start | bytes 1572872 | tf_op jit(solution)/shard_map/ppermute | solution.py:47
  149.6 28.4 %collective-permute-start.2 = (bf16[8,2,128,128]{3,2,0,1:T(8,128)(2,1)S(1)}, bf16[8,2,128,128]{3,2,0,1:T(8,128)(2,1)S(1)}, u32[]{:S(2)}, u32[]{:S(2)}) collective-permute-start(bf16[8,2,128,128]{3,2,0,1:T(8,128)(2,1)S(1)} %collective-permute-done.1), channel_id=1, source_target_pairs={{0,224},{32,0},{64,32},{96,64},{128,96},{160,128},{192,160},{224,1... | collective-permute-start | bytes 1572872 | tf_op jit(solution)/shard_map/ppermute | solution.py:46
  175.9 14.8 %collective-permute-start.6 = (bf16[4,2,128,128]{3,2,0,1:T(8,128)(2,1)S(1)}, bf16[4,2,128,128]{3,2,0,1:T(8,128)(2,1)S(1)}, u32[]{:S(2)}, u32[]{:S(2)}) collective-permute-start(bf16[4,2,128,128]{3,2,0,1:T(8,128)(2,1)S(1)} %slice.72), channel_id=1, source_target_pairs={{0,32},{32,64},{64,96},{96,128},{128,160},{160,192},{192,224},{224... | collective-permute-start | bytes 786440 | tf_op jit(solution)/shard_map/ppermute | solution.py:52
  178.0 13.5 %collective-permute-start.7 = (bf16[4,2,128,128]{3,2,0,1:T(8,128)(2,1)S(1)}, bf16[4,2,128,128]{3,2,0,1:T(8,128)(2,1)S(1)}, u32[]{:S(2)}, u32[]{:S(2)}) collective-permute-start(bf16[4,2,128,128]{3,2,0,1:T(8,128)(2,1)S(1)} %slice.73), channel_id=1, source_target_pairs={{0,224},{32,0},{64,32},{96,64},{128,96},{160,128},{192,160},{224,1... | collective-permute-start | bytes 786440 | tf_op jit(solution)/shard_map/ppermute | solution.py:53
  207.4 1.6 copy-start.3
  207.4 3.1 copy-start.6
  209.0 3.2 copy-start.2
  244.1 88.4 %reduce-scatter.5.cloned.1.call-start = ((), (), s32[]{:S(2)}) async-start(), calls=%async_computation.9 | async-start | bytes 1179648 | tf_op jit(solution)/shard_map/reduce_scatter | solution.py:162
  290.8 3.0 copy-start.5
  293.9 2.6 copy-start.4
  296.5 36.0 %copy-start.1 = (bf16[4096,256]{1,0:T(8,128)(2,1)S(1)}, bf16[4096,256]{1,0:T(8,128)(2,1)}, u32[]{:S(2)}) copy-start(bf16[4096,256]{1,0:T(8,128)(2,1)} %param.12) | copy-start | bytes 6291460
Sparse Core Ops, SparseCore 0:
  100.8 90.5 all-gather.1
  291.0 41.4 reduce-scatter.4
Sparse Core Ops, SparseCore 1:
  244.2 19.9 reduce-scatter.2
